TPU v7x, 32 devices: a whole 2x2x4 slice. The times are simulated.
32 devices in a mesh: space: 4 (over z), vel: 8 (over y, x, core).
Axes of the slice: x: 2, y: 2, z: 4, core: 2. Of those that a mesh axis runs over, the one named last changes fastest.
Arguments:
- distribution: bfloat16 [4096, 24, 8, 128], P('vel', 'space'), may hold values from -6 to 6
- up_factor: bfloat16 [4096, 256], P('vel'), may hold values from -0.75 to 0.75
- down_factor: bfloat16 [4096, 256], P('vel'), may hold values from -0.09375 to 0.09375
- decay: float32 [4096], P('vel'), may hold values from 0.3 to 3
- wall_kind: int32 [2, 8, 128], replicated, may hold values from 0 to 2
Outputs:
- advanced: bfloat16 [4096, 24, 8, 128], P('vel', 'space')
Inputs may be any that keep to these rules, and one draw needn't show every extreme that they name: `wall_kind`: 0 marks a diffuse wall at rest, 1 a diffuse heated wall, 2 an open face.
All inputs are finite; a program needn't handle non-finite values.
Results may differ from a plain program's by a relative error of at most 0.0046.
Values may be sent and summed in bfloat16 or wider, within the bound.
No kernel may reach another device: no remote copies, remote signals or barrier semaphores. Data moves between devices by JAX's collectives and lax.ppermute only.
A program may use at most 192 MiB of HBM per device.

v0:
```python
import jax
import jax.numpy as jnp
from jax import lax
from jax.sharding import PartitionSpec as P

NV = 16
STEPS = 2


speed_range = 8.0
time_ratio = 0.08
wall_heat = 3.0


def with_halo(block, sides, width):
    for axis, dim in sides:
        count = lax.axis_size(axis)
        forward = [(i, i + 1) for i in range(count - 1)]
        backward = [(target, source) for source, target in forward]
        low = lax.ppermute(
            lax.slice_in_dim(block, block.shape[dim] - width, None, axis=dim), axis, forward
        )
        high = lax.ppermute(lax.slice_in_dim(block, 0, width, axis=dim), axis, backward)
        block = jnp.concatenate([low, block, high], axis=dim)
    return block


def components(vel_ids):
    spacing = speed_range / NV
    midpoint = (NV - 1) / 2.0
    along_z = ((vel_ids // (NV * NV)).astype(jnp.float32) - midpoint) * spacing
    along_x = ((vel_ids // NV % NV).astype(jnp.float32) - midpoint) * spacing
    along_y = ((vel_ids % NV).astype(jnp.float32) - midpoint) * spacing
    return (along_z, along_x, along_y)


def wall_ghost(outflux, kind_face, maxwell, energy, norm):
    sigma = outflux / norm
    heating = jnp.where(kind_face == 1, wall_heat, 0.0)
    opened = jnp.where(kind_face == 2, 0.0, 1.0)
    return (
        maxwell[:, None, None]
        * (sigma[None] + heating[None] * energy[:, None, None])
        * opened[None]
    )


def transport(centre, lower_plane, upper_plane, along_z, along_x, along_y):
    dimensions = centre.ndim
    shaped = (-1,) + (1,) * (dimensions - 1)
    axis_x = dimensions - 2
    axis_y = dimensions - 1
    plus_z = jnp.maximum(along_z, 0.0).reshape(shaped)
    minus_z = jnp.minimum(along_z, 0.0).reshape(shaped)
    plus_x = jnp.maximum(along_x, 0.0).reshape(shaped)
    minus_x = jnp.minimum(along_x, 0.0).reshape(shaped)
    plus_y = jnp.maximum(along_y, 0.0).reshape(shaped)
    minus_y = jnp.minimum(along_y, 0.0).reshape(shaped)
    result = plus_z * (centre - lower_plane) + minus_z * (upper_plane - centre)
    result = (
        result
        + plus_x * (centre - jnp.roll(centre, 1, axis_x))
        + minus_x * (jnp.roll(centre, -1, axis_x) - centre)
    )
    result = (
        result
        + plus_y * (centre - jnp.roll(centre, 1, axis_y))
        + minus_y * (jnp.roll(centre, -1, axis_y) - centre)
    )
    return result


def body(distribution, up_factor, down_factor, decay, wall_kind):
    local_vel, depth, width_x, width_y = distribution.shape
    cells = depth * width_x * width_y
    vel_ids = lax.axis_index("vel") * local_vel + jnp.arange(local_vel, dtype=jnp.int32)
    along_z, along_x, along_y = components(vel_ids)
    speed_sq = along_z * along_z + along_x * along_x + along_y * along_y
    maxwell = jnp.exp(-0.5 * speed_sq)
    energy = 0.5 * speed_sq - 1.5
    all_ids = jnp.arange(NV**3, dtype=jnp.int32)
    full_z, full_x, full_y = components(all_ids)
    norm = jnp.sum(
        jnp.maximum(full_z, 0.0)
        * jnp.exp(-0.5 * (full_z * full_z + full_x * full_x + full_y * full_y))
    )
    slab = lax.axis_index("space")
    slabs = lax.axis_size("space")
    current = distribution
    for step in range(STEPS):
        low_face = current[:, 0].astype(jnp.float32)
        high_face = current[:, depth - 1].astype(jnp.float32)
        out_low = jnp.sum(jnp.maximum(-along_z, 0.0)[:, None, None] * low_face, axis=0)
        out_high = jnp.sum(jnp.maximum(along_z, 0.0)[:, None, None] * high_face, axis=0)
        outflux = lax.psum(jnp.stack([out_low, out_high]), "vel")
        ghost_low = wall_ghost(outflux[0], wall_kind[0], maxwell, energy, norm)
        ghost_high = wall_ghost(outflux[1], wall_kind[1], maxwell, energy, norm)
        padded = with_halo(current, (("space", 1),), 1)
        first_plane = jnp.where(slab == 0, ghost_low, padded[:, 0].astype(jnp.float32))
        last_plane = jnp.where(
            slab == slabs - 1, ghost_high, padded[:, depth + 1].astype(jnp.float32)
        )
        lower_plane = jnp.concatenate(
            [first_plane[:, None], padded[:, 1:depth].astype(jnp.float32)], axis=1
        )
        upper_plane = jnp.concatenate(
            [padded[:, 2 : depth + 1].astype(jnp.float32), last_plane[:, None]], axis=1
        )
        centre = current.astype(jnp.float32)
        moved = transport(centre, lower_plane, upper_plane, along_z, along_x, along_y)
        flat_rows = current.reshape(local_vel, cells)
        coeffs = lax.psum_scatter(
            lax.dot_general(
                flat_rows, down_factor, (((0,), (0,)), ((), ())), preferred_element_type=jnp.float32
            ),
            "vel",
            scatter_dimension=0,
            tiled=True,
        ).astype(jnp.bfloat16)
        gained = lax.dot_general(
            up_factor,
            lax.all_gather(coeffs, "vel", axis=0, tiled=True),
            (((1,), (1,)), ((), ())),
            preferred_element_type=jnp.float32,
        ).reshape(current.shape)
        updated = (
            centre
            - time_ratio * moved
            + time_ratio * (gained - decay[:, None, None, None] * centre)
        )
        current = updated.astype(jnp.bfloat16)
    return current


def solution(mesh):
    return jax.shard_map(
        body,
        mesh=mesh,
        in_specs=(P("vel", "space", None, None), P("vel", None), P("vel", None), P("vel"), P()),
        out_specs=P("vel", "space", None, None),
        check_vma=False,
    )
```

profile of v0, /device:TPU:0, one launch (start us, length us, event | category | flops | bytes accessed | tf_op | source)
XLA Modules:
  0.0 400.8 jit_solution(969379979568579661)
XLA Ops:
  6.5 8.9 %fusion.35 = f32[6144,256]{1,0:T(8,128)} fusion(bf16[512,256]{1,0:T(8,128)(2,1)} %param.7, bf16[64,8,48,128]{3,2,1,0:T(8,128)(2,1)} %bitcast.78), kind=kOutput, calls=%fused_computation.51 | convolution fusion | flops 1610612736 | bytes 12845056 | tf_op jit(solution)/shard_map/dot_general | solution.py:113
  15.5 0.0 reduce-scatter.3.cloned.1.call-update
  15.5 0.0 all-gather.3.cloned.1.call-start
  15.6 3.1 slice_bitcast_fusion.2
  18.6 6.0 %collective-permute-start = (bf16[512,1,8,128]{3,2,0,1:T(8,128)(2,1)}, bf16[512,1,8,128]{3,2,0,1:T(8,128)(2,1)}, u32[]{:S(2)}, u32[]{:S(2)}) collective-permute-start(bf16[512,1,8,128]{3,2,0,1:T(8,128)(2,1)} %get-tuple-element.21), channel_id=1, source_target_pairs={{0,8},{8,16},{16,24},{1,9},{9,17},{17,25},{2,10},{10,18},{18,26},{... | collective-permute-start | bytes 3145736 | tf_op jit(solution)/shard_map/ppermute | solution.py:20
  24.7 1.3 collective-permute-start.1
  26.0 3.7 fusion.57
  29.7 13.6 %psum.14 = f32[2,8,128]{2,1,0:T(8,128)S(1)} all-reduce(f32[2,8,128]{2,1,0:T(8,128)S(1)} %pad_maximum_fusion), channel_id=1, replica_groups=mesh['space'=4,'vel'=8] {'vel'}, use_global_device_ids=true, to_apply=%region_2.3 | all-reduce | flops 2048 | bytes 16384 | tf_op jit(solution)/shard_map/psum | solution.py:95
  43.3 0.7 fusion.86
  44.0 0.6 fusion.90
  44.7 35.4 %reduce-scatter.3.cloned.1.call-done = f32[768,256]{1,0:T(8,128)} async-done(((f32[6144,256]{1,0:T(8,128)}), f32[768,256]{1,0:T(8,128)}) %reduce-scatter.3.cloned.1.call-update) | async-done | bytes 786448 | tf_op jit(solution)/shard_map/reduce_scatter | solution.py:112
  80.1 1.9 convert_element_type.151
  82.1 0.0 all-gather.3.cloned.1.call-update
  82.1 0.2 reduce-scatter.5.cloned.1.call-start
  82.3 0.0 slice-start.2
  82.3 13.6 %fusion.112 = (f32[512,6,8,127]{3,2,1,0:T(8,128)}, f32[512,6,8,127]{3,2,1,0:T(8,128)}) fusion(bf16[512,6,8,128]{3,2,1,0:T(8,128)(2,1)} %param.5), kind=kLoop, calls=%fused_computation.186 | loop fusion | bytes 49938432 | tf_op jit(solution)/shard_map/jit(_roll_static)/slice | solution.py:67
  96.0 13.2 %fusion.111 = (f32[512,6,8,1]{3,2,1,0:T(8,128)}, f32[512,6,8,1]{3,2,1,0:T(8,128)}) fusion(bf16[512,6,8,128]{3,2,1,0:T(8,128)(2,1)} %param.5), kind=kLoop, calls=%fused_computation.185 | loop fusion | bytes 393216 | tf_op jit(solution)/shard_map/jit(_roll_static)/slice | solution.py:67
  109.2 9.0 %fusion.110 = (f32[512,6,7,128]{3,2,1,0:T(8,128)}, f32[512,6,7,128]{3,2,1,0:T(8,128)}) fusion(bf16[512,6,8,128]{3,2,1,0:T(8,128)(2,1)S(1)} %bitcast.80), kind=kLoop, calls=%fused_computation.184 | loop fusion | bytes 44040192 | tf_op jit(solution)/shard_map/jit(_roll_static)/slice | solution.py:62
  118.2 3.1 fusion.109
  121.3 12.4 %slice_convert_fusion.3 = (f32[512,5,8,128]{3,2,1,0:T(8,128)}, f32[512,5,8,128]{3,2,1,0:T(8,128)}) fusion(bf16[512,6,8,128]{3,2,1,0:T(8,128)(2,1)} %param.5), kind=kLoop, calls=%fused_computation.57 | loop fusion | flops 5242880 | bytes 31457280 | tf_op jit(solution)/shard_map/convert_element_type | solution.py:104
  133.7 4.5 %fusion.41 = f32[512,1,8,128]{3,2,1,0:T(8,128)} fusion(bf16[512,1,8,128]{3,2,0,1:T(8,128)(2,1)} %collective-permute-done, f32[8,128]{1,0:T(8,128)S(1)} %get-tuple-element.38, f32[512]{0:T(512)S(1)} %get-tuple-element.43, f32[8,128]{1,0:T(8,128)S(1)} %get-tuple-element.37, f32[8,128]{1,0:T(8,128)S(1)} %get-tuple-element.35, f32[512]{0:T(512)S(1)} %get-tuple-element.44, ...), kind=kLoop, calls=%fused_computation.65 | loop fusion | flops 3145728 | bytes 3162113 | tf_op jit(solution)/shard_map/jit(_where)/select_n | solution.py:99
  138.2 0.0 collective-permute-done.1
  138.2 3.1 fusion.49
  141.3 8.3 %fusion.113 = f32[6144,512]{1,0:T(8,128)} fusion(bf16[6144,256]{1,0:T(8,128)(2,1)} %all-gather.3.cloned.1.call-done, bf16[512,256]{1,0:T(8,128)(2,1)S(1)} %copy-done), kind=kOutput, calls=%fused_computation.187 | convolution fusion | flops 1610612736 | bytes 15990784 | tf_op jit(solution)/shard_map/dot_general | solution.py:120
  149.6 12.6 %copy.10 = f32[512,6,8,128]{3,2,1,0:T(8,128)} copy(f32[512,6,8,128]{0,3,2,1:T(8,128)} %bitcast.81) | data formatting | bytes 25165824 | tf_op jit(solution)/shard_map/reshape | solution.py:125
  162.3 40.6 %fusion.31 = bf16[512,6,8,128]{3,2,1,0:T(8,128)(2,1)S(1)} fusion(f32[512,6,8,128]{3,2,1,0:T(8,128)} %copy.10, f32[512,6,8,1]{3,2,1,0:T(8,128)} %get-tuple-element.30, f32[512,6,8,127]{3,2,1,0:T(8,128)} %get-tuple-element.32, f32[512,6,8,127]{3,2,1,0:T(8,128)} %get-tuple-element.31, f32[512,6,8,1]{3,2,1,0:T(8,128)} %get-tuple-element.29, ...), kind=kLoop, calls=%fused_computation.47 | loop fusion | flops 97517568 | bytes 100677632 | tf_op jit(solution)/shard_map/convert_element_type | solution.py:131
  202.9 2.6 copy-done.1
  205.5 7.0 %fusion.32 = f32[6144,256]{1,0:T(8,128)} fusion(bf16[512,256]{1,0:T(8,128)(2,1)} %param.7, bf16[64,8,48,128]{3,2,1,0:T(8,128)(2,1)S(1)} %bitcast.75), kind=kOutput, calls=%fused_computation.48 | convolution fusion | flops 1610612736 | bytes 12845056 | tf_op jit(solution)/shard_map/dot_general | solution.py:113
  212.6 0.0 reduce-scatter.5.cloned.1.call-update
  212.6 0.0 all-gather.5.cloned.1.call-start
  212.6 3.0 slice_bitcast_fusion
  215.7 3.4 collective-permute-start.2
  219.1 1.3 collective-permute-start.3
  220.4 3.7 fusion.55
  224.1 12.3 %psum.15 = f32[2,8,128]{2,1,0:T(8,128)S(1)} all-reduce(f32[2,8,128]{2,1,0:T(8,128)S(1)} %pad_maximum_fusion.1), channel_id=1, replica_groups=mesh['space'=4,'vel'=8] {'vel'}, use_global_device_ids=true, to_apply=%region_7.8 | all-reduce | flops 2048 | bytes 16384 | tf_op jit(solution)/shard_map/psum | solution.py:95
  236.5 38.0 %reduce-scatter.5.cloned.1.call-done = f32[768,256]{1,0:T(8,128)} async-done(((f32[6144,256]{1,0:T(8,128)}), f32[768,256]{1,0:T(8,128)}) %reduce-scatter.5.cloned.1.call-update) | async-done | bytes 786448 | tf_op jit(solution)/shard_map/reduce_scatter | solution.py:112
  274.5 1.9 convert_element_type.162
  276.4 0.0 all-gather.5.cloned.1.call-update
  276.4 12.9 %slice_convert_fusion.1 = (f32[512,5,8,128]{3,2,1,0:T(8,128)}, f32[512,5,8,128]{3,2,1,0:T(8,128)}) fusion(bf16[512,6,8,128]{3,2,1,0:T(8,128)(2,1)} %copy-done.1), kind=kLoop, calls=%fused_computation.55 | loop fusion | flops 5242880 | bytes 31457280 | tf_op jit(solution)/shard_map/convert_element_type | solution.py:104
  289.4 13.6 %fusion.108 = (f32[512,6,8,127]{3,2,1,0:T(8,128)}, f32[512,6,8,127]{3,2,1,0:T(8,128)}) fusion(bf16[512,6,8,128]{3,2,1,0:T(8,128)(2,1)} %copy-done.1), kind=kLoop, calls=%fused_computation.182 | loop fusion | bytes 49938432 | tf_op jit(solution)/shard_map/jit(_roll_static)/slice | solution.py:67
  303.0 9.0 %fusion.106 = (f32[512,6,7,128]{3,2,1,0:T(8,128)}, f32[512,6,7,128]{3,2,1,0:T(8,128)}) fusion(bf16[512,6,8,128]{3,2,1,0:T(8,128)(2,1)S(1)} %bitcast.77), kind=kLoop, calls=%fused_computation.180 | loop fusion | bytes 44040192 | tf_op jit(solution)/shard_map/jit(_roll_static)/slice | solution.py:62
  312.1 9.3 %fusion.107 = (f32[512,6,8,1]{3,2,1,0:T(8,128)}, f32[512,6,8,1]{3,2,1,0:T(8,128)}) fusion(bf16[512,6,8,128]{3,2,1,0:T(8,128)(2,1)S(1)} %bitcast.77), kind=kLoop, calls=%fused_computation.181 | loop fusion | bytes 393216 | tf_op jit(solution)/shard_map/jit(_roll_static)/slice | solution.py:67
  321.3 0.6 fusion.88
  322.0 3.6 fusion.105
  325.6 4.8 %fusion.45 = (f32[512,1,8,128]{3,2,1,0:T(8,128)S(1)}, f32[512,1,8,128]{3,2,1,0:T(8,128)}) fusion(bf16[512,1,8,128]{3,2,0,1:T(8,128)(2,1)S(1)} %collective-permute-done.2, f32[8,128]{1,0:T(8,128)S(1)} %get-tuple-element.33, f32[8,128]{1,0:T(8,128)S(1)} %get-tuple-element.38, f32[512]{0:T(512)S(1)} %get-tuple-element.43, f32[8,128]{1,0:T(8,128)S(1)} %get-tuple-element.37, ...), kind=kLoop, calls=%fused_computation.69 | loop fusion | flops 6291456 | bytes 6320130 | tf_op jit(solution)/shard_map/jit(_where)/select_n | solution.py:99
  330.3 8.3 %fusion.114 = f32[6144,512]{1,0:T(8,128)} fusion(bf16[6144,256]{1,0:T(8,128)(2,1)} %all-gather.5.cloned.1.call-done, bf16[512,256]{1,0:T(8,128)(2,1)S(1)} %copy-done), kind=kOutput, calls=%fused_computation.188 | convolution fusion | flops 1610612736 | bytes 15990784 | tf_op jit(solution)/shard_map/dot_general | solution.py:120
  338.6 12.6 %copy.15 = f32[512,6,8,128]{3,2,1,0:T(8,128)} copy(f32[512,6,8,128]{0,3,2,1:T(8,128)} %bitcast.82) | data formatting | bytes 25165824 | tf_op jit(solution)/shard_map/reshape | solution.py:125
  351.3 42.5 %fusion.30 = bf16[512,6,8,128]{3,2,1,0:T(8,128)(2,1)} fusion(f32[512,6,8,128]{3,2,1,0:T(8,128)} %copy.15, f32[512,6,8,1]{3,2,1,0:T(8,128)} %get-tuple-element.18, f32[512,6,8,127]{3,2,1,0:T(8,128)} %get-tuple-element.20, f32[512,6,8,127]{3,2,1,0:T(8,128)} %get-tuple-element.19, f32[512,6,8,1]{3,2,1,0:T(8,128)} %get-tuple-element.17, ...), kind=kLoop, calls=%fused_computation.46 | loop fusion | flops 97517568 | bytes 100677632 | tf_op jit(solution)/shard_map/convert_element_type | solution.py:131
  (30 shorter events, 0.2 us)
Async XLA Ops:
  6.5 134.8 %copy-start = (bf16[512,256]{1,0:T(8,128)(2,1)S(1)}, bf16[512,256]{1,0:T(8,128)(2,1)}, u32[]{:S(2)}) copy-start(bf16[512,256]{1,0:T(8,128)(2,1)} %param.6) | copy-start | bytes 786436
  6.5 73.6 %reduce-scatter.3.cloned.1.call-start = ((), (), s32[]{:S(2)}) async-start(), calls=%async_computation.2 | async-start | bytes 7077888 | tf_op jit(solution)/shard_map/reduce_scatter | solution.py:112
  6.5 38.1 %copy-start.2 = (s32[2,8,128]{2,1,0:T(8,128)S(1)}, s32[2,8,128]{2,1,0:T(8,128)}, u32[]{:S(2)}) copy-start(s32[2,8,128]{2,1,0:T(8,128)} %param.9) | copy-start | bytes 24580
  15.5 125.8 %all-gather.3.cloned.1.call-start = ((), (), s32[]{:S(2)}) async-start(), calls=%async_computation.3 | async-start | bytes 3538944 | tf_op jit(solution)/shard_map/all_gather | solution.py:122
  18.6 115.1 %collective-permute-start = (bf16[512,1,8,128]{3,2,0,1:T(8,128)(2,1)}, bf16[512,1,8,128]{3,2,0,1:T(8,128)(2,1)}, u32[]{:S(2)}, u32[]{:S(2)}) collective-permute-start(bf16[512,1,8,128]{3,2,0,1:T(8,128)(2,1)} %get-tuple-element.21), channel_id=1, source_target_pairs={{0,8},{8,16},{16,24},{1,9},{9,17},{17,25},{2,10},{10,18},{18,26},{... | collective-permute-start | bytes 3145736 | tf_op jit(solution)/shard_map/ppermute | solution.py:20
  24.7 113.6 %collective-permute-start.1 = (bf16[512,1,8,128]{3,2,1,0:T(8,128)(2,1)}, bf16[512,1,8,128]{3,2,1,0:T(8,128)(2,1)S(1)}, u32[]{:S(2)}, u32[]{:S(2)}) collective-permute-start(bf16[512,1,8,128]{3,2,1,0:T(8,128)(2,1)} %get-tuple-element.22), channel_id=1, source_target_pairs={{8,0},{16,8},{24,16},{9,1},{17,9},{25,17},{10,2},{18,10},{26,18},{... | collective-permute-start | bytes 3145736 | tf_op jit(solution)/shard_map/ppermute | solution.py:23
  82.1 192.4 %reduce-scatter.5.cloned.1.call-start = ((), (), s32[]{:S(2)}) async-start(), calls=%async_computation.4 | async-start | bytes 7077888 | tf_op jit(solution)/shard_map/reduce_scatter | solution.py:112
  82.3 26.8 %slice-start.2 = ((s8[6291456]{0:T(1024)(128)(4,1)}), s8[4194304]{0:T(1024)(128)(4,1)S(1)}, s32[]{:S(2)}) async-start(s8[6291456]{0:T(1024)(128)(4,1)} %bitcast.79), calls=%async_computation.8 | async-start | bytes 8388608
  96.0 13.2 %slice-start.3 = ((s8[6291456]{0:T(1024)(128)(4,1)}), s8[2097152]{0:T(1024)(128)(4,1)S(1)}, s32[]{:S(2)}) async-start(s8[6291456]{0:T(1024)(128)(4,1)} %bitcast.79), calls=%async_computation.9 | async-start | bytes 4194304
  149.6 12.6 %copy-start.3 = (f32[512]{0:T(512)S(1)}, f32[512]{0:T(512)}, u32[]{:S(2)}) copy-start(f32[512]{0:T(512)} %param.8) | copy-start | bytes 6148
  202.9 2.6 copy-start.1
  212.6 117.7 %all-gather.5.cloned.1.call-start = ((), (), s32[]{:S(2)}) async-start(), calls=%async_computation.5 | async-start | bytes 3538944 | tf_op jit(solution)/shard_map/all_gather | solution.py:122
  215.7 109.9 %collective-permute-start.2 = (bf16[512,1,8,128]{3,2,0,1:T(8,128)(2,1)}, bf16[512,1,8,128]{3,2,0,1:T(8,128)(2,1)S(1)}, u32[]{:S(2)}, u32[]{:S(2)}) collective-permute-start(bf16[512,1,8,128]{3,2,0,1:T(8,128)(2,1)} %get-tuple-element.9), channel_id=1, source_target_pairs={{0,8},{8,16},{16,24},{1,9},{9,17},{17,25},{2,10},{10,18},{18,26},{... | collective-permute-start | bytes 3145736 | tf_op jit(solution)/shard_map/ppermute | solution.py:20
  219.1 106.4 %collective-permute-start.3 = (bf16[512,1,8,128]{3,2,0,1:T(8,128)(2,1)}, bf16[512,1,8,128]{3,2,0,1:T(8,128)(2,1)}, u32[]{:S(2)}, u32[]{:S(2)}) collective-permute-start(bf16[512,1,8,128]{3,2,0,1:T(8,128)(2,1)} %get-tuple-element.10), channel_id=1, source_target_pairs={{8,0},{16,8},{24,16},{9,1},{17,9},{25,17},{10,2},{18,10},{26,18},{... | collective-permute-start | bytes 3145736 | tf_op jit(solution)/shard_map/ppermute | solution.py:23
  276.4 26.6 %slice-start = ((s8[6291456]{0:T(1024)(128)(4,1)}), s8[2097152]{0:T(1024)(128)(4,1)S(1)}, s32[]{:S(2)}) async-start(s8[6291456]{0:T(1024)(128)(4,1)} %bitcast.76), calls=%async_computation.6 | async-start | bytes 4194304
  289.4 13.7 %slice-start.1 = ((s8[6291456]{0:T(1024)(128)(4,1)}), s8[4194304]{0:T(1024)(128)(4,1)S(1)}, s32[]{:S(2)}) async-start(s8[6291456]{0:T(1024)(128)(4,1)} %bitcast.76), calls=%async_computation.7 | async-start | bytes 8388608
Sparse Core Ops, SparseCore 0:
  15.6 64.4 reduce-scatter.2
  82.2 32.1 all-gather.2
  212.7 61.7 reduce-scatter.4
  276.5 32.1 all-gather.4
where the time goes:
time: 406 us; the launch traced here: 401 us
  other arithmetic  134 us (33%)
  local copies, waits for them, and re-layouts  109 us (27%)
  waiting for transfers between devices  73.5 us (18%)
  matrix products  32.5 us (8%)
  blocking collectives  25.9 us (6%)
  between operations  13.8 us (3%)
  starting transfers between devices  12.3 us (3%)
    convert_element_type x2, other arithmetic, body(): current = updated.astype(jnp.bfloat16)  83.2 us
    reduce_scatter x2, waiting for transfers between devices, body(): lax.psum_scatter(lax.dot_general(flat_rows, down_factor, (((0,), (0,)), (...  73.4 us
    slice x4, local copies, waits for them, and re-layouts, transport(): jnp.roll(centre, 1, axis_y)  49.7 us
    psum x2, blocking collectives, body(): outflux = lax.psum(jnp.stack([out_low, out_high]), 'vel')  25.9 us
    convert_element_type x2, other arithmetic, body(): padded[:, 1:depth].astype(jnp.float32)  25.3 us
    reshape x2, local copies, waits for them, and re-layouts, body(): gained = lax.dot_general(up_factor, lax.all_gather(coeffs, 'vel', axis=0,...  25.3 us
    slice x4, local copies, waits for them, and re-layouts, transport(): jnp.roll(centre, 1, axis_x)  24.7 us
    dot_general x2, matrix products, body(): lax.dot_general(up_factor, lax.all_gather(coeffs, 'vel', axis=0, tiled=Tr...  16.6 us
  transfers between devices with their start and end apart: 8, of which 2 were waited for; matrix products, arithmetic and copies ran while one was open for 33% of the time, Pallas kernels for 0%

commit v1 on v0

v1 whole, which is shorter than its diff:
```python
import functools

import jax
import jax.numpy as jnp
from jax import lax
from jax.experimental import pallas as pl
from jax.experimental.pallas import tpu as pltpu
from jax.sharding import PartitionSpec as P

NV = 16
STEPS = 2


speed_range = 8.0
time_ratio = 0.08
wall_heat = 3.0


def components(vel_ids):
    spacing = speed_range / NV
    midpoint = (NV - 1) / 2.0
    along_z = ((vel_ids // (NV * NV)).astype(jnp.float32) - midpoint) * spacing
    along_x = ((vel_ids // NV % NV).astype(jnp.float32) - midpoint) * spacing
    along_y = ((vel_ids % NV).astype(jnp.float32) - midpoint) * spacing
    return (along_z, along_x, along_y)


def wall_ghost(outflux, kind_face, maxwell, energy, norm):
    sigma = outflux / norm
    heating = jnp.where(kind_face == 1, wall_heat, 0.0)
    opened = jnp.where(kind_face == 2, 0.0, 1.0)
    return (
        maxwell[:, None]
        * (sigma[None] + heating[None] * energy[:, None])
        * opened[None]
    )


def update_kernel(par_ref, up_ref, coef_ref, cur_ref, lo_ref, hi_ref, out_ref, work_ref, *, depth, plane, width):
    work_ref[:, 0:plane] = lo_ref[...]
    work_ref[:, (depth + 1) * plane:(depth + 2) * plane] = hi_ref[...]
    work_ref[:, plane:(depth + 1) * plane] = cur_ref[...].astype(jnp.float32)
    rows = plane // width
    up = up_ref[...]

    def one_plane(z, carry):
        base = pl.multiple_of((z + 1) * plane, plane)
        gained = jnp.dot(
            up, coef_ref[:, pl.ds(pl.multiple_of(z * plane, plane), plane)],
            preferred_element_type=jnp.float32,
        )
        for x in range(rows):
            at = base + x * width
            xm = base + ((x - 1) % rows) * width
            xp = base + ((x + 1) % rows) * width
            c = work_ref[:, pl.ds(at, width)]
            lo = work_ref[:, pl.ds(at - plane, width)]
            hi = work_ref[:, pl.ds(at + plane, width)]
            left = work_ref[:, pl.ds(xm, width)]
            right = work_ref[:, pl.ds(xp, width)]
            down_y = pltpu.roll(c, 1, 1)
            up_y = pltpu.roll(c, width - 1, 1)
            total = (
                par_ref[0] * c
                + par_ref[1] * lo
                + par_ref[2] * hi
                + par_ref[3] * left
                + par_ref[4] * right
                + par_ref[5] * down_y
                + par_ref[6] * up_y
                + time_ratio * gained[:, x * width:(x + 1) * width]
            )
            out_ref[:, pl.ds(pl.multiple_of(z * plane + x * width, width), width)] = total.astype(out_ref.dtype)
        return carry

    lax.fori_loop(0, depth, one_plane, 0)


def body(distribution, up_factor, down_factor, decay, wall_kind):
    local_vel, depth, width_x, width_y = distribution.shape
    plane = width_x * width_y
    cells = depth * plane
    rank = up_factor.shape[1]
    vel_ids = lax.axis_index("vel") * local_vel + jnp.arange(local_vel, dtype=jnp.int32)
    along_z, along_x, along_y = components(vel_ids)
    speed_sq = along_z * along_z + along_x * along_x + along_y * along_y
    maxwell = jnp.exp(-0.5 * speed_sq)
    energy = 0.5 * speed_sq - 1.5
    all_ids = jnp.arange(NV**3, dtype=jnp.int32)
    full_z, full_x, full_y = components(all_ids)
    norm = jnp.sum(
        jnp.maximum(full_z, 0.0)
        * jnp.exp(-0.5 * (full_z * full_z + full_x * full_x + full_y * full_y))
    )
    slab = lax.axis_index("space")
    slabs = lax.axis_size("space")
    dt = time_ratio
    per_vel = jnp.stack(
        [
            1.0 - dt * (jnp.abs(along_z) + jnp.abs(along_x) + jnp.abs(along_y)) - dt * decay,
            dt * jnp.maximum(along_z, 0.0),
            -dt * jnp.minimum(along_z, 0.0),
            dt * jnp.maximum(along_x, 0.0),
            -dt * jnp.minimum(along_x, 0.0),
            dt * jnp.maximum(along_y, 0.0),
            -dt * jnp.minimum(along_y, 0.0),
        ]
    )
    params = jnp.broadcast_to(per_vel[:, :, None], (7, local_vel, width_y))
    wl = jnp.maximum(-along_z, 0.0)
    wh = jnp.maximum(along_z, 0.0)
    count = slabs
    forward = [(i, i + 1) for i in range(count - 1)]
    backward = [(i + 1, i) for i in range(count - 1)]

    vb = 128
    kernel = functools.partial(update_kernel, depth=depth, plane=plane, width=width_y)
    update = pl.pallas_call(
        kernel,
        grid=(local_vel // vb,),
        in_specs=[
            pl.BlockSpec((7, vb, width_y), lambda i: (0, i, 0)),
            pl.BlockSpec((vb, rank), lambda i: (i, 0)),
            pl.BlockSpec((rank, cells), lambda i: (0, 0)),
            pl.BlockSpec((vb, cells), lambda i: (i, 0)),
            pl.BlockSpec((vb, plane), lambda i: (i, 0)),
            pl.BlockSpec((vb, plane), lambda i: (i, 0)),
        ],
        out_specs=pl.BlockSpec((vb, cells), lambda i: (i, 0)),
        out_shape=jax.ShapeDtypeStruct((local_vel, cells), jnp.bfloat16),
        scratch_shapes=[pltpu.VMEM((vb, cells + 2 * plane), jnp.float32)],
        compiler_params=pltpu.CompilerParams(vmem_limit_bytes=48 * 1024 * 1024),
    )

    current = distribution.reshape(local_vel, cells)
    for step in range(STEPS):
        low_face = current[:, :plane]
        high_face = current[:, cells - plane:]
        out_low = jnp.sum(wl[:, None] * low_face.astype(jnp.float32), axis=0)
        out_high = jnp.sum(wh[:, None] * high_face.astype(jnp.float32), axis=0)
        outflux = lax.psum(jnp.stack([out_low, out_high]), "vel")
        ghost_low = wall_ghost(outflux[0], wall_kind[0].reshape(plane), maxwell, energy, norm)
        ghost_high = wall_ghost(outflux[1], wall_kind[1].reshape(plane), maxwell, energy, norm)
        from_below = lax.ppermute(high_face, "space", forward)
        from_above = lax.ppermute(low_face, "space", backward)
        lower_plane = jnp.where(slab == 0, ghost_low, from_below.astype(jnp.float32))
        upper_plane = jnp.where(slab == slabs - 1, ghost_high, from_above.astype(jnp.float32))
        partial = lax.dot_general(
            down_factor, current, (((0,), (0,)), ((), ())), preferred_element_type=jnp.float32
        )
        coeffs = lax.psum_scatter(partial, "vel", scatter_dimension=1, tiled=True).astype(jnp.bfloat16)
        coeffs = lax.all_gather(coeffs, "vel", axis=1, tiled=True)
        current = update(params, up_factor, coeffs, current, lower_plane, upper_plane)
    return current.reshape(local_vel, depth, width_x, width_y)


def solution(mesh):
    return jax.shard_map(
        body,
        mesh=mesh,
        in_specs=(P("vel", "space", None, None), P("vel", None), P("vel", None), P("vel"), P()),
        out_specs=P("vel", "space", None, None),
        check_vma=False,
    )
```

time: 406 us -> 290 us (0.71); the launches traced: 401 us -> 290 us
  other arithmetic: 134 us -> 17.4 us
  local copies, waits for them, and re-layouts: 109 us -> 23.8 us
  waiting for transfers between devices: 73.5 us -> 139 us
  Pallas kernels: 0 us -> 43.2 us
  matrix products: 32.5 us -> 14.8 us
    convert_element_type x6 -> x2, other arithmetic: 112 us -> 3.84 us  [body(): lax.psum_scatter(partial, 'vel', scatter_dimension=1, tiled=True)]
    slice x8 -> x2, local copies, waits for them, and re-layouts: 74.4 us -> 4.57 us  [body(): low_face = current[:, :plane]]
    reduce_scatter x2, waiting for transfers between devices: 73.4 us -> 127 us  [body(): lax.psum_scatter(partial, 'vel', scatter_dimension=1, tiled=True)]
    pallas_call x0 -> x2, Pallas kernels: none -> 43.2 us  [body(): update(params, up_factor, coeffs, current, lower_plane, upper_plane)]
    reshape x2 -> x0, local copies, waits for them, and re-layouts: 25.3 us -> none  [body(): gained = lax.dot_general(up_factor, lax.all_gather(coeffs, 'vel', axis=0,...]
    dot_general x4 -> x2, matrix products: 32.5 us -> 14.8 us  [body(): lax.dot_general(down_factor, current, (((0,), (0,)), ((), ())), preferred...]
    ppermute x4, waiting for transfers between devices: 0.01 us -> 11.2 us  [the longest x2 8.67 us: body(): from_above = lax.ppermute(low_face, 'space', backward)]
    unnamed x18, local copies, waits for them, and re-layouts: 8.78 us -> 18.7 us
  transfers between devices with their start and end apart: 8 -> 8, of which waited for: 2 -> 6; matrix products, arithmetic and copies ran while one was open for 33% -> 8% of each run, Pallas kernels for 0% -> 0%
where the time goes in v1:
time: 290 us
  waiting for transfers between devices  139 us (48%)
  Pallas kernels  43.2 us (15%)
  blocking collectives  25.7 us (9%)
  local copies, waits for them, and re-layouts  23.8 us (8%)
  other arithmetic  17.4 us (6%)
  matrix products  14.8 us (5%)
  between operations  13.3 us (5%)
  starting transfers between devices  13 us (4%)
    reduce_scatter x2, waiting for transfers between devices, body(): lax.psum_scatter(partial, 'vel', scatter_dimension=1, tiled=True)  127 us
    pallas_call x2, Pallas kernels, body(): update(params, up_factor, coeffs, current, lower_plane, upper_plane)  43.2 us
    psum x2, blocking collectives, body(): outflux = lax.psum(jnp.stack([out_low, out_high]), 'vel')  25.7 us
    unnamed x18, local copies, waits for them, and re-layouts  18.7 us
    dot_general x2, matrix products, body(): lax.dot_general(down_factor, current, (((0,), (0,)), ((), ())), preferred...  14.8 us
    ppermute x2, starting transfers between devices, body(): from_below = lax.ppermute(high_face, 'space', forward)  10.2 us
    ppermute x2, waiting for transfers between devices, body(): from_above = lax.ppermute(low_face, 'space', backward)  8.67 us
    select_n x2, other arithmetic, body(): jnp.where(slab == slabs - 1, ghost_high, from_above.astype(jnp.float32))  7.25 us
  transfers between devices with their start and end apart: 8, of which 6 were waited for; matrix products, arithmetic and copies ran while one was open for 8% of the time, Pallas kernels for 0%

profile of v1, /device:TPU:0, one launch (start us, length us, event | category | flops | bytes accessed | tf_op | source)
XLA Modules:
  0.0 289.7 jit_solution(4354774756244726844)
XLA Ops:
  6.5 0.0 copy-start
  6.5 0.0 reduce-scatter.3.cloned.1.call-start
  6.5 0.9 copy-done
  7.5 7.4 %fusion.64 = f32[256,6144]{1,0:T(8,128)} fusion(bf16[512,256]{1,0:T(8,128)(2,1)S(1)} %copy-done, bf16[64,8,48,128]{3,2,1,0:T(8,128)(2,1)} %bitcast.34), kind=kOutput, calls=%fused_computation.132 | convolution fusion | flops 1610612736 | bytes 12845056 | tf_op jit(solution)/shard_map/dot_general | solution.py:148
  14.9 0.0 reduce-scatter.3.cloned.1.call-update
  14.9 0.0 all-gather.3.cloned.1.call-start
  15.0 64.5 %reduce-scatter.3.cloned.1.call-done = f32[256,768]{1,0:T(8,128)} async-done(((f32[256,6144]{1,0:T(8,128)}), f32[256,768]{1,0:T(8,128)}) %reduce-scatter.3.cloned.1.call-update) | async-done | bytes 786448 | tf_op jit(solution)/shard_map/reduce_scatter | solution.py:151
  79.5 1.9 convert_element_type.120
  81.4 0.0 all-gather.3.cloned.1.call-update
  81.4 0.0 reduce-scatter.5.cloned.1.call-start
  81.5 4.4 %copy.12 = bf16[64,8,48,128]{3,1,2,0:T(8,128)(2,1)S(1)} copy(bf16[64,8,48,128]{3,2,1,0:T(8,128)(2,1)} %bitcast.35) | data formatting | bytes 12582912
  85.9 0.0 copy-start.5
  85.9 2.7 copy-done.5
  88.6 1.5 fusion.66
  90.1 1.4 collective-permute-start.1
  91.5 4.6 %collective-permute-start = (bf16[512,1024]{1,0:T(8,128)(2,1)}, bf16[512,1024]{1,0:T(8,128)(2,1)S(1)}, u32[]{:S(2)}, u32[]{:S(2)}) collective-permute-start(bf16[512,1024]{1,0:T(8,128)(2,1)} %get-tuple-element.12), channel_id=1, source_target_pairs={{0,8},{8,16},{16,24},{1,9},{9,17},{17,25},{2,10},{10,18},{18,26},{... | collective-permute-start | bytes 3145736 | tf_op jit(solution)/shard_map/ppermute | solution.py:144
  96.2 0.0 copy-done.7
  96.3 2.0 multiply_reduce_fusion.3
  98.4 13.0 %psum.14 = f32[2,1024]{1,0:T(2,128)S(1)} all-reduce(f32[2,1024]{1,0:T(2,128)S(1)} %pad_maximum_fusion), channel_id=1, replica_groups=mesh['space'=4,'vel'=8] {'vel'}, use_global_device_ids=true, to_apply=%region_3.4 | all-reduce | flops 2048 | bytes 16384 | tf_op jit(solution)/shard_map/psum | solution.py:141
  111.4 0.7 fusion.40
  112.1 0.7 slice_divide_fusion.2
  112.8 0.0 copy-done.6
  112.9 4.2 %collective-permute-done.1 = bf16[512,1024]{1,0:T(8,128)(2,1)S(1)} collective-permute-done((bf16[512,1024]{1,0:T(8,128)(2,1)}, bf16[512,1024]{1,0:T(8,128)(2,1)S(1)}, u32[]{:S(2)}, u32[]{:S(2)}) %collective-permute-start.1) | collective-permute-done | bytes 1048608 | tf_op jit(solution)/shard_map/ppermute | solution.py:145
  117.1 1.3 collective-permute-done
  118.4 3.0 %fusion.8 = (f32[512,1024]{1,0:T(8,128)}, f32[512,1024]{1,0:T(8,128)}) fusion(bf16[512,1024]{1,0:T(8,128)(2,1)S(1)} %collective-permute-done.1, f32[1024]{0:T(1024)S(1)} %get-tuple-element.19, f32[1024]{0:T(1024)S(1)} %get-tuple-element.17, f32[1024]{0:T(1024)S(1)} %bitcast.39, f32[512]{0:T(512)S(1)} %get-tuple-element.25, f32[512]{0:T(512)S(1)} %get-tuple-element.26, ...), kind=kLoop, calls=%fused_computation.14 | loop fusion | flops 6291456 | bytes 6320130 | tf_op jit(solution)/shard_map/jit(_where)/select_n | solution.py:147
  121.3 0.5 broadcast_in_dim.26.par_ref
  121.9 0.0 copy-done.4
  121.9 0.0 copy-start.3
  121.9 1.6 copy-done.3
  123.5 21.6 %shard_map.55.cur_ref = bf16[512,6144]{1,0:T(8,128)(2,1)} custom-call(f32[7,512,128]{2,1,0:T(8,128)S(1)} %broadcast_in_dim.26.par_ref, bf16[512,256]{1,0:T(8,128)(2,1)S(1)} %copy-done.4, bf16[256,6144]{1,0:T(8,128)(2,1)} %all-gather.3.cloned.1.call-done.coef_ref, bf16[512,6144]{1,0:T(8,128)(2,1)} %bitcast.33, f32[512,1024]{1,0:T(8,128)S(1)} %copy-done.3, ...), custom_call_target="tpu_custom_call" | custom-call | tf_op jit(solution)/shard_map/pallas_call | solution.py:153
  145.1 7.3 %convolution_bitcast_fusion = f32[256,6144]{1,0:T(8,128)} fusion(bf16[512,6144]{1,0:T(8,128)(2,1)} %shard_map.55.cur_ref, bf16[512,256]{1,0:T(8,128)(2,1)S(1)} %copy-done), kind=kOutput, calls=%fused_computation | convolution fusion | flops 1610612736 | bytes 12845056 | tf_op jit(solution)/shard_map/dot_general | solution.py:148
  152.4 0.0 reduce-scatter.5.cloned.1.call-update
  152.4 0.0 all-gather.5.cloned.1.call-start
  152.5 62.7 %reduce-scatter.5.cloned.1.call-done = f32[256,768]{1,0:T(8,128)} async-done(((f32[256,6144]{1,0:T(8,128)}), f32[256,768]{1,0:T(8,128)}) %reduce-scatter.5.cloned.1.call-update) | async-done | bytes 786448 | tf_op jit(solution)/shard_map/reduce_scatter | solution.py:151
  215.2 1.9 convert_element_type.128
  217.1 0.0 all-gather.5.cloned.1.call-update
  217.1 3.1 %fusion.65 = (bf16[512,1024]{1,0:T(8,128)(2,1)}, bf16[512,1024]{1,0:T(8,128)(2,1)}) fusion(bf16[512,6144]{1,0:T(8,128)(2,1)} %shard_map.55.cur_ref), kind=kLoop, calls=%fused_computation.133 | loop fusion | bytes 4194304 | tf_op jit(solution)/shard_map/slice | solution.py:137
  220.2 1.3 collective-permute-start.3
  221.5 5.6 %collective-permute-start.2 = (bf16[512,1024]{1,0:T(8,128)(2,1)}, bf16[512,1024]{1,0:T(8,128)(2,1)}, u32[]{:S(2)}, u32[]{:S(2)}) collective-permute-start(bf16[512,1024]{1,0:T(8,128)(2,1)} %get-tuple-element.10), channel_id=1, source_target_pairs={{0,8},{8,16},{16,24},{1,9},{9,17},{17,25},{2,10},{10,18},{18,26},{... | collective-permute-start | bytes 3145736 | tf_op jit(solution)/shard_map/ppermute | solution.py:144
  227.1 2.0 multiply_reduce_fusion.1
  229.1 12.7 %psum.15 = f32[2,1024]{1,0:T(2,128)S(1)} all-reduce(f32[2,1024]{1,0:T(2,128)S(1)} %pad_maximum_fusion.1), channel_id=1, replica_groups=mesh['space'=4,'vel'=8] {'vel'}, use_global_device_ids=true, to_apply=%region_8.9 | all-reduce | flops 2048 | bytes 16384 | tf_op jit(solution)/shard_map/psum | solution.py:141
  241.9 0.7 slice_divide_fusion
  242.6 4.5 %collective-permute-done.3 = bf16[512,1024]{1,0:T(8,128)(2,1)S(1)} collective-permute-done((bf16[512,1024]{1,0:T(8,128)(2,1)}, bf16[512,1024]{1,0:T(8,128)(2,1)S(1)}, u32[]{:S(2)}, u32[]{:S(2)}) %collective-permute-start.3) | collective-permute-done | bytes 1048608 | tf_op jit(solution)/shard_map/ppermute | solution.py:145
  247.0 1.3 collective-permute-done.2
  248.3 4.3 %fusion.11 = (f32[512,1024]{1,0:T(8,128)}, f32[512,1024]{1,0:T(8,128)}) fusion(bf16[512,1024]{1,0:T(8,128)(2,1)S(1)} %collective-permute-done.3, f32[1024]{0:T(1024)S(1)} %bitcast.37, f32[1024]{0:T(1024)S(1)} %get-tuple-element.19, f32[1024]{0:T(1024)S(1)} %get-tuple-element.17, f32[512]{0:T(512)S(1)} %get-tuple-element.25, f32[512]{0:T(512)S(1)} %get-tuple-element.26, ...), kind=kLoop, calls=%fused_computation.17 | loop fusion | flops 6291456 | bytes 6320130 | tf_op jit(solution)/shard_map/jit(_where)/select_n | solution.py:147
  252.6 1.6 copy-done.2
  254.2 21.6 %shard_map.56 = bf16[512,6144]{1,0:T(8,128)(2,1)} custom-call(f32[7,512,128]{2,1,0:T(8,128)S(1)} %broadcast_in_dim.26.par_ref, bf16[512,256]{1,0:T(8,128)(2,1)S(1)} %copy-done.4, bf16[256,6144]{1,0:T(8,128)(2,1)} %all-gather.5.cloned.1.call-done.coef_ref, bf16[512,6144]{1,0:T(8,128)(2,1)} %shard_map.55.cur_ref, f32[512,1024]{1,0:T(8,128)S(1)} %copy-done.2, ...), custom_call_target="tpu_custom_call" | custom-call | tf_op jit(solution)/shard_map/pallas_call | solution.py:153
  275.8 7.4 %copy.9 = bf16[64,8,48,128]{3,2,1,0:T(8,128)(2,1)} copy(bf16[64,8,48,128]{3,1,2,0:T(8,128)(2,1)} %bitcast.36) | data formatting | bytes 12582912
  (18 shorter events, 0.2 us)
Async XLA Ops:
  6.5 1.0 copy-start
  6.5 72.9 %reduce-scatter.3.cloned.1.call-start = ((), (), s32[]{:S(2)}) async-start(), calls=%async_computation.2 | async-start | bytes 7077888 | tf_op jit(solution)/shard_map/reduce_scatter | solution.py:151
  14.9 106.4 %all-gather.3.cloned.1.call-start = ((), (), s32[]{:S(2)}) async-start(), calls=%async_computation.3 | async-start | bytes 3538944 | tf_op jit(solution)/shard_map/all_gather | solution.py:152
  81.4 133.8 %reduce-scatter.5.cloned.1.call-start = ((), (), s32[]{:S(2)}) async-start(), calls=%async_computation.4 | async-start | bytes 7077888 | tf_op jit(solution)/shard_map/reduce_scatter | solution.py:151
  85.9 2.7 copy-start.5
  88.6 7.6 %copy-start.7 = (f32[512]{0:T(512)S(1)}, f32[512]{0:T(512)}, u32[]{:S(2)}) copy-start(f32[512]{0:T(512)} %param.8) | copy-start | bytes 6148
  90.1 22.7 %copy-start.6 = (s32[2,8,128]{2,1,0:T(8,128)S(1)}, s32[2,8,128]{2,1,0:T(8,128)}, u32[]{:S(2)}) copy-start(s32[2,8,128]{2,1,0:T(8,128)} %param.9) | copy-start | bytes 24580
  90.1 27.0 %collective-permute-start.1 = (bf16[512,1024]{1,0:T(8,128)(2,1)}, bf16[512,1024]{1,0:T(8,128)(2,1)S(1)}, u32[]{:S(2)}, u32[]{:S(2)}) collective-permute-start(bf16[512,1024]{1,0:T(8,128)(2,1)} %get-tuple-element.11), channel_id=1, source_target_pairs={{8,0},{16,8},{24,16},{9,1},{17,9},{25,17},{10,2},{18,10},{26,18},{... | collective-permute-start | bytes 3145736 | tf_op jit(solution)/shard_map/ppermute | solution.py:145
  91.5 26.8 %collective-permute-start = (bf16[512,1024]{1,0:T(8,128)(2,1)}, bf16[512,1024]{1,0:T(8,128)(2,1)S(1)}, u32[]{:S(2)}, u32[]{:S(2)}) collective-permute-start(bf16[512,1024]{1,0:T(8,128)(2,1)} %get-tuple-element.12), channel_id=1, source_target_pairs={{0,8},{8,16},{16,24},{1,9},{9,17},{17,25},{2,10},{10,18},{18,26},{... | collective-permute-start | bytes 3145736 | tf_op jit(solution)/shard_map/ppermute | solution.py:144
  118.4 3.5 %copy-start.4 = (bf16[512,256]{1,0:T(8,128)(2,1)S(1)}, bf16[512,256]{1,0:T(8,128)(2,1)}, u32[]{:S(2)}) copy-start(bf16[512,256]{1,0:T(8,128)(2,1)} %up_ref.3) | copy-start | bytes 786436
  121.9 1.6 copy-start.3
  152.4 100.2 %all-gather.5.cloned.1.call-start = ((), (), s32[]{:S(2)}) async-start(), calls=%async_computation.5 | async-start | bytes 3538944 | tf_op jit(solution)/shard_map/all_gather | solution.py:152
  220.2 26.9 %collective-permute-start.3 = (bf16[512,1024]{1,0:T(8,128)(2,1)}, bf16[512,1024]{1,0:T(8,128)(2,1)S(1)}, u32[]{:S(2)}, u32[]{:S(2)}) collective-permute-start(bf16[512,1024]{1,0:T(8,128)(2,1)} %get-tuple-element.9), channel_id=1, source_target_pairs={{8,0},{16,8},{24,16},{9,1},{17,9},{25,17},{10,2},{18,10},{26,18},{... | collective-permute-start | bytes 3145736 | tf_op jit(solution)/shard_map/ppermute | solution.py:145
  221.5 26.9 %collective-permute-start.2 = (bf16[512,1024]{1,0:T(8,128)(2,1)}, bf16[512,1024]{1,0:T(8,128)(2,1)}, u32[]{:S(2)}, u32[]{:S(2)}) collective-permute-start(bf16[512,1024]{1,0:T(8,128)(2,1)} %get-tuple-element.10), channel_id=1, source_target_pairs={{0,8},{8,16},{16,24},{1,9},{9,17},{17,25},{2,10},{10,18},{18,26},{... | collective-permute-start | bytes 3145736 | tf_op jit(solution)/shard_map/ppermute | solution.py:144
  252.6 1.6 copy-start.2
  275.8 7.4 %copy-start.1 = (bf16[512,256]{1,0:T(8,128)(2,1)S(1)}, bf16[512,256]{1,0:T(8,128)(2,1)}, u32[]{:S(2)}) copy-start(bf16[512,256]{1,0:T(8,128)(2,1)} %param.7) | copy-start | bytes 786436
Sparse Core Ops, SparseCore 0:
  15.0 64.3 reduce-scatter.2
  81.5 32.4 all-gather.2
  152.5 62.5 reduce-scatter.4
  217.2 32.3 all-gather.4

commit v2 on v1

--- a/solution.py
+++ b/solution.py
@@ -138,7 +138,7 @@
         high_face = current[:, cells - plane:]
         out_low = jnp.sum(wl[:, None] * low_face.astype(jnp.float32), axis=0)
         out_high = jnp.sum(wh[:, None] * high_face.astype(jnp.float32), axis=0)
-        outflux = lax.psum(jnp.stack([out_low, out_high]), "vel")
+        outflux = jnp.sum(lax.all_gather(jnp.stack([out_low, out_high]), "vel"), axis=0)
         ghost_low = wall_ghost(outflux[0], wall_kind[0].reshape(plane), maxwell, energy, norm)
         ghost_high = wall_ghost(outflux[1], wall_kind[1].reshape(plane), maxwell, energy, norm)
         from_below = lax.ppermute(high_face, "space", forward)
@@ -147,9 +147,9 @@
         upper_plane = jnp.where(slab == slabs - 1, ghost_high, from_above.astype(jnp.float32))
         partial = lax.dot_general(
             down_factor, current, (((0,), (0,)), ((), ())), preferred_element_type=jnp.float32
-        )
-        coeffs = lax.psum_scatter(partial, "vel", scatter_dimension=1, tiled=True).astype(jnp.bfloat16)
-        coeffs = lax.all_gather(coeffs, "vel", axis=1, tiled=True)
+        ).astype(jnp.bfloat16)
+        coeffs = lax.psum_scatter(partial, "vel", scatter_dimension=0, tiled=True)
+        coeffs = lax.all_gather(coeffs, "vel", axis=0, tiled=True)
         current = update(params, up_factor, coeffs, current, lower_plane, upper_plane)
     return current.reshape(local_vel, depth, width_x, width_y)
 

time: 290 us -> 253 us (0.87)
  waiting for transfers between devices: 139 us -> 114 us
  blocking collectives: 25.7 us -> 18.6 us
  other arithmetic: 17.4 us -> 13.5 us
    reduce_scatter x2, waiting for transfers between devices: 127 us -> 96 us  [body(): coeffs = lax.psum_scatter(partial, 'vel', scatter_dimension=0, tiled=True)]
    psum x2 -> x0, blocking collectives: 25.7 us -> none  [body(): outflux = lax.psum(jnp.stack([out_low, out_high]), 'vel')]
    all_gather x0 -> x2, blocking collectives: none -> 18.6 us  [body(): lax.all_gather(jnp.stack([out_low, out_high]), 'vel')]
    ppermute x2, waiting for transfers between devices: 8.67 us -> 15.8 us  [body(): from_above = lax.ppermute(low_face, 'space', backward)]
    convert_element_type x2 -> x0, other arithmetic: 3.84 us -> none  [body(): lax.psum_scatter(partial, 'vel', scatter_dimension=1, tiled=True)]
    unnamed x18 -> x16, local copies, waits for them, and re-layouts: 18.7 us -> 18.6 us
  transfers between devices with their start and end apart: 8 -> 8, of which waited for: 6 -> 6; matrix products, arithmetic and copies ran while one was open for 8% -> 9% of each run, Pallas kernels for 0% -> 0%
where the time goes in v2:
time: 253 us
  waiting for transfers between devices  114 us (45%)
  Pallas kernels  43.2 us (17%)
  local copies, waits for them, and re-layouts  23.8 us (9%)
  blocking collectives  18.6 us (7%)
  other arithmetic  13.5 us (5%)
  between operations  13.3 us (5%)
  starting transfers between devices  13 us (5%)
  matrix products  12.7 us (5%)
    reduce_scatter x2, waiting for transfers between devices, body(): coeffs = lax.psum_scatter(partial, 'vel', scatter_dimension=0, tiled=True)  96 us
    pallas_call x2, Pallas kernels, body(): update(params, up_factor, coeffs, current, lower_plane, upper_plane)  43.2 us
    unnamed x16, local copies, waits for them, and re-layouts  18.6 us
    all_gather x2, blocking collectives, body(): lax.all_gather(jnp.stack([out_low, out_high]), 'vel')  18.6 us
    ppermute x2, waiting for transfers between devices, body(): from_above = lax.ppermute(low_face, 'space', backward)  15.8 us
    dot_general x2, matrix products, body(): lax.dot_general(down_factor, current, (((0,), (0,)), ((), ())), preferred...  12.7 us
    ppermute x2, starting transfers between devices, body(): from_below = lax.ppermute(high_face, 'space', forward)  10.2 us
    select_n x2, other arithmetic, body(): jnp.where(slab == slabs - 1, ghost_high, from_above.astype(jnp.float32))  7.22 us
  transfers between devices with their start and end apart: 8, of which 6 were waited for; matrix products, arithmetic and copies ran while one was open for 9% of the time, Pallas kernels for 0%

profile of v2, /device:TPU:0, one launch (start us, length us, event | category | flops | bytes accessed | tf_op | source)
XLA Modules:
  0.0 252.5 jit_solution(6911012895600317582)
XLA Ops:
  6.5 0.0 copy-start
  6.5 0.0 reduce-scatter.3.cloned.1.call-start
  6.5 0.9 copy-done
  7.5 6.4 %convolution_convert_fusion.1 = bf16[256,6144]{1,0:T(8,128)(2,1)} fusion(bf16[512,256]{1,0:T(8,128)(2,1)S(1)} %copy-done, bf16[64,8,48,128]{3,2,1,0:T(8,128)(2,1)} %bitcast.38), kind=kOutput, calls=%fused_computation.1 | convolution fusion | flops 1612185600 | bytes 9699328 | tf_op jit(solution)/shard_map/dot_general | solution.py:148
  13.9 0.0 reduce-scatter.3.cloned.1.call-update
  13.9 0.0 all-gather.7.cloned.1.call-start
  13.9 48.9 %reduce-scatter.3.cloned.1.call-done = bf16[32,6144]{1,0:T(8,128)(2,1)} async-done(((bf16[256,6144]{1,0:T(8,128)(2,1)}), bf16[32,6144]{1,0:T(8,128)(2,1)}) %reduce-scatter.3.cloned.1.call-update) | async-done | bytes 393232 | tf_op jit(solution)/shard_map/reduce_scatter | solution.py:151
  62.8 0.0 all-gather.7.cloned.1.call-update
  62.8 0.0 reduce-scatter.5.cloned.1.call-start
  62.9 4.4 %copy.13 = bf16[64,8,48,128]{3,1,2,0:T(8,128)(2,1)S(1)} copy(bf16[64,8,48,128]{3,2,1,0:T(8,128)(2,1)} %bitcast.39) | data formatting | bytes 12582912
  67.3 0.0 copy-start.4
  67.3 2.7 %copy-done.4 = bf16[64,8,48,128]{3,1,2,0:T(8,128)(2,1)} copy-done((bf16[64,8,48,128]{3,1,2,0:T(8,128)(2,1)}, bf16[64,8,48,128]{3,1,2,0:T(8,128)(2,1)S(1)}, u32[]{:S(2)}) %copy-start.4) | copy-done | bytes 6291480
  70.0 1.5 fusion.66
  71.5 0.0 copy-start.5
  71.5 1.4 collective-permute-start.1
  73.0 4.6 %collective-permute-start = (bf16[512,1024]{1,0:T(8,128)(2,1)}, bf16[512,1024]{1,0:T(8,128)(2,1)S(1)}, u32[]{:S(2)}, u32[]{:S(2)}) collective-permute-start(bf16[512,1024]{1,0:T(8,128)(2,1)} %get-tuple-element.12), channel_id=1, source_target_pairs={{0,8},{8,16},{16,24},{1,9},{9,17},{17,25},{2,10},{10,18},{18,26},{... | collective-permute-start | bytes 3145736 | tf_op jit(solution)/shard_map/ppermute | solution.py:144
  77.6 2.0 multiply_reduce_fusion.3
  79.7 9.2 %all-gather.2 = f32[8,2,1024]{2,1,0:T(2,128)S(1)} all-gather(f32[1,2,1024]{2,1,0:T(2,128)S(1)} %maximum_bitcast_fusion), channel_id=2, replica_groups=mesh['space'=4,'vel'=8] {'vel'}, dimensions={0}, use_global_device_ids=true | all-gather | bytes 73728 | tf_op jit(solution)/shard_map/all_gather | solution.py:141
  89.0 0.0 copy-done.6
  89.1 0.7 fusion.41
  89.8 0.6 slice_divide_fusion.2
  90.4 0.0 copy-done.5
  90.5 8.0 %collective-permute-done.1 = bf16[512,1024]{1,0:T(8,128)(2,1)S(1)} collective-permute-done((bf16[512,1024]{1,0:T(8,128)(2,1)}, bf16[512,1024]{1,0:T(8,128)(2,1)S(1)}, u32[]{:S(2)}, u32[]{:S(2)}) %collective-permute-start.1) | collective-permute-done | bytes 1048608 | tf_op jit(solution)/shard_map/ppermute | solution.py:145
  98.5 1.3 collective-permute-done
  99.8 0.0 copy-start.3
  99.8 3.0 %fusion.9 = (f32[512,1024]{1,0:T(8,128)}, f32[512,1024]{1,0:T(8,128)}) fusion(bf16[512,1024]{1,0:T(8,128)(2,1)S(1)} %collective-permute-done.1, f32[1024]{0:T(1024)S(1)} %get-tuple-element.19, f32[1024]{0:T(1024)S(1)} %get-tuple-element.17, f32[1024]{0:T(1024)S(1)} %bitcast.43, f32[512]{0:T(512)S(1)} %get-tuple-element.25, f32[512]{0:T(512)S(1)} %get-tuple-element.26, ...), kind=kLoop, calls=%fused_computation.16 | loop fusion | flops 6291456 | bytes 6320130 | tf_op jit(solution)/shard_map/jit(_where)/select_n | solution.py:147
  102.7 0.5 broadcast_in_dim.26.par_ref
  103.3 0.0 copy-done.3
  103.3 0.0 copy-start.2
  103.3 1.6 copy-done.2
  104.9 21.6 %shard_map.55.cur_ref = bf16[512,6144]{1,0:T(8,128)(2,1)} custom-call(f32[7,512,128]{2,1,0:T(8,128)S(1)} %broadcast_in_dim.26.par_ref, bf16[512,256]{1,0:T(8,128)(2,1)S(1)} %copy-done.3, bf16[256,6144]{1,0:T(8,128)(2,1)} %all-gather.7.cloned.1.call-done.coef_ref, bf16[512,6144]{1,0:T(8,128)(2,1)} %bitcast.37, f32[512,1024]{1,0:T(8,128)S(1)} %copy-done.2, ...), custom_call_target="tpu_custom_call" | custom-call | tf_op jit(solution)/shard_map/pallas_call | solution.py:153
  126.5 6.3 %fusion = bf16[256,6144]{1,0:T(8,128)(2,1)} fusion(bf16[512,6144]{1,0:T(8,128)(2,1)} %shard_map.55.cur_ref, bf16[512,256]{1,0:T(8,128)(2,1)S(1)} %copy-done), kind=kOutput, calls=%fused_computation.2 | convolution fusion | flops 1612185600 | bytes 9699328 | tf_op jit(solution)/shard_map/dot_general | solution.py:148
  132.8 0.0 reduce-scatter.5.cloned.1.call-update
  132.8 0.0 all-gather.9.cloned.1.call-start
  132.8 47.1 %reduce-scatter.5.cloned.1.call-done = bf16[32,6144]{1,0:T(8,128)(2,1)} async-done(((bf16[256,6144]{1,0:T(8,128)(2,1)}), bf16[32,6144]{1,0:T(8,128)(2,1)}) %reduce-scatter.5.cloned.1.call-update) | async-done | bytes 393232 | tf_op jit(solution)/shard_map/reduce_scatter | solution.py:151
  180.0 0.0 all-gather.9.cloned.1.call-update
  180.0 3.1 %fusion.65 = (bf16[512,1024]{1,0:T(8,128)(2,1)}, bf16[512,1024]{1,0:T(8,128)(2,1)}) fusion(bf16[512,6144]{1,0:T(8,128)(2,1)} %shard_map.55.cur_ref), kind=kLoop, calls=%fused_computation.134 | loop fusion | bytes 4194304 | tf_op jit(solution)/shard_map/slice | solution.py:137
  183.1 1.3 collective-permute-start.3
  184.3 5.6 %collective-permute-start.2 = (bf16[512,1024]{1,0:T(8,128)(2,1)}, bf16[512,1024]{1,0:T(8,128)(2,1)}, u32[]{:S(2)}, u32[]{:S(2)}) collective-permute-start(bf16[512,1024]{1,0:T(8,128)(2,1)} %get-tuple-element.10), channel_id=1, source_target_pairs={{0,8},{8,16},{16,24},{1,9},{9,17},{17,25},{2,10},{10,18},{18,26},{... | collective-permute-start | bytes 3145736 | tf_op jit(solution)/shard_map/ppermute | solution.py:144
  190.0 2.0 multiply_reduce_fusion.1
  192.0 9.4 %all-gather.3 = f32[8,2,1024]{2,1,0:T(2,128)S(1)} all-gather(f32[1,2,1024]{2,1,0:T(2,128)S(1)} %maximum_bitcast_fusion.1), channel_id=3, replica_groups=mesh['space'=4,'vel'=8] {'vel'}, dimensions={0}, use_global_device_ids=true | all-gather | bytes 73728 | tf_op jit(solution)/shard_map/all_gather | solution.py:141
  201.5 0.6 slice_divide_fusion
  202.1 7.8 %collective-permute-done.3 = bf16[512,1024]{1,0:T(8,128)(2,1)S(1)} collective-permute-done((bf16[512,1024]{1,0:T(8,128)(2,1)}, bf16[512,1024]{1,0:T(8,128)(2,1)S(1)}, u32[]{:S(2)}, u32[]{:S(2)}) %collective-permute-start.3) | collective-permute-done | bytes 1048608 | tf_op jit(solution)/shard_map/ppermute | solution.py:145
  209.9 1.3 collective-permute-done.2
  211.2 4.2 %fusion.12 = (f32[512,1024]{1,0:T(8,128)}, f32[512,1024]{1,0:T(8,128)}) fusion(bf16[512,1024]{1,0:T(8,128)(2,1)S(1)} %collective-permute-done.3, f32[1024]{0:T(1024)S(1)} %bitcast.41, f32[1024]{0:T(1024)S(1)} %get-tuple-element.19, f32[1024]{0:T(1024)S(1)} %get-tuple-element.17, f32[512]{0:T(512)S(1)} %get-tuple-element.25, f32[512]{0:T(512)S(1)} %get-tuple-element.26, ...), kind=kLoop, calls=%fused_computation.19 | loop fusion | flops 6291456 | bytes 6320130 | tf_op jit(solution)/shard_map/jit(_where)/select_n | solution.py:147
  215.4 1.6 copy-done.1
  217.0 21.6 %shard_map.56 = bf16[512,6144]{1,0:T(8,128)(2,1)} custom-call(f32[7,512,128]{2,1,0:T(8,128)S(1)} %broadcast_in_dim.26.par_ref, bf16[512,256]{1,0:T(8,128)(2,1)S(1)} %copy-done.3, bf16[256,6144]{1,0:T(8,128)(2,1)} %all-gather.9.cloned.1.call-done.coef_ref, bf16[512,6144]{1,0:T(8,128)(2,1)} %shard_map.55.cur_ref, f32[512,1024]{1,0:T(8,128)S(1)} %copy-done.1, ...), custom_call_target="tpu_custom_call" | custom-call | tf_op jit(solution)/shard_map/pallas_call | solution.py:153
  238.6 7.4 %copy.10 = bf16[64,8,48,128]{3,2,1,0:T(8,128)(2,1)} copy(bf16[64,8,48,128]{3,1,2,0:T(8,128)(2,1)} %bitcast.40) | data formatting | bytes 12582912
  (16 shorter events, 0.3 us)
Async XLA Ops:
  6.5 1.0 copy-start
  6.5 56.3 %reduce-scatter.3.cloned.1.call-start = ((), (), s32[]{:S(2)}) async-start(), calls=%async_computation.2 | async-start | bytes 3538944 | tf_op jit(solution)/shard_map/reduce_scatter | solution.py:151
  13.9 88.9 %all-gather.7.cloned.1.call-start = ((), (), s32[]{:S(2)}) async-start(), calls=%async_computation.3 | async-start | bytes 3538944 | tf_op jit(solution)/shard_map/all_gather | solution.py:152
  62.8 117.1 %reduce-scatter.5.cloned.1.call-start = ((), (), s32[]{:S(2)}) async-start(), calls=%async_computation.4 | async-start | bytes 3538944 | tf_op jit(solution)/shard_map/reduce_scatter | solution.py:151
  67.3 2.7 %copy-start.4 = (bf16[64,8,48,128]{3,1,2,0:T(8,128)(2,1)}, bf16[64,8,48,128]{3,1,2,0:T(8,128)(2,1)S(1)}, u32[]{:S(2)}) copy-start(bf16[64,8,48,128]{3,1,2,0:T(8,128)(2,1)S(1)} %copy.13) | copy-start | bytes 18874372
  71.5 17.5 %copy-start.6 = (f32[512]{0:T(512)S(1)}, f32[512]{0:T(512)}, u32[]{:S(2)}) copy-start(f32[512]{0:T(512)} %param.8) | copy-start | bytes 6148
  71.5 18.9 %copy-start.5 = (s32[2,8,128]{2,1,0:T(8,128)S(1)}, s32[2,8,128]{2,1,0:T(8,128)}, u32[]{:S(2)}) copy-start(s32[2,8,128]{2,1,0:T(8,128)} %param.9) | copy-start | bytes 24580
  71.5 26.9 %collective-permute-start.1 = (bf16[512,1024]{1,0:T(8,128)(2,1)}, bf16[512,1024]{1,0:T(8,128)(2,1)S(1)}, u32[]{:S(2)}, u32[]{:S(2)}) collective-permute-start(bf16[512,1024]{1,0:T(8,128)(2,1)} %get-tuple-element.11), channel_id=1, source_target_pairs={{8,0},{16,8},{24,16},{9,1},{17,9},{25,17},{10,2},{18,10},{26,18},{... | collective-permute-start | bytes 3145736 | tf_op jit(solution)/shard_map/ppermute | solution.py:145
  73.0 26.8 %collective-permute-start = (bf16[512,1024]{1,0:T(8,128)(2,1)}, bf16[512,1024]{1,0:T(8,128)(2,1)S(1)}, u32[]{:S(2)}, u32[]{:S(2)}) collective-permute-start(bf16[512,1024]{1,0:T(8,128)(2,1)} %get-tuple-element.12), channel_id=1, source_target_pairs={{0,8},{8,16},{16,24},{1,9},{9,17},{17,25},{2,10},{10,18},{18,26},{... | collective-permute-start | bytes 3145736 | tf_op jit(solution)/shard_map/ppermute | solution.py:144
  99.8 3.5 %copy-start.3 = (bf16[512,256]{1,0:T(8,128)(2,1)S(1)}, bf16[512,256]{1,0:T(8,128)(2,1)}, u32[]{:S(2)}) copy-start(bf16[512,256]{1,0:T(8,128)(2,1)} %up_ref.3) | copy-start | bytes 786436
  103.3 1.6 copy-start.2
  132.8 82.6 %all-gather.9.cloned.1.call-start = ((), (), s32[]{:S(2)}) async-start(), calls=%async_computation.5 | async-start | bytes 3538944 | tf_op jit(solution)/shard_map/all_gather | solution.py:152
  183.1 26.8 %collective-permute-start.3 = (bf16[512,1024]{1,0:T(8,128)(2,1)}, bf16[512,1024]{1,0:T(8,128)(2,1)S(1)}, u32[]{:S(2)}, u32[]{:S(2)}) collective-permute-start(bf16[512,1024]{1,0:T(8,128)(2,1)} %get-tuple-element.9), channel_id=1, source_target_pairs={{8,0},{16,8},{24,16},{9,1},{17,9},{25,17},{10,2},{18,10},{26,18},{... | collective-permute-start | bytes 3145736 | tf_op jit(solution)/shard_map/ppermute | solution.py:145
  184.3 26.8 %collective-permute-start.2 = (bf16[512,1024]{1,0:T(8,128)(2,1)}, bf16[512,1024]{1,0:T(8,128)(2,1)}, u32[]{:S(2)}, u32[]{:S(2)}) collective-permute-start(bf16[512,1024]{1,0:T(8,128)(2,1)} %get-tuple-element.10), channel_id=1, source_target_pairs={{0,8},{8,16},{16,24},{1,9},{9,17},{17,25},{2,10},{10,18},{18,26},{... | collective-permute-start | bytes 3145736 | tf_op jit(solution)/shard_map/ppermute | solution.py:144
  215.4 1.6 copy-start.1
Sparse Core Ops, SparseCore 0:
  14.0 48.7 reduce-scatter.2
  64.7 32.2 all-gather.6
  132.9 47.0 reduce-scatter.4
  181.7 32.3 all-gather.8
